TPU v7x, 512 devices: a whole 4x4x16 slice. The times are simulated.
512 devices in a mesh: tm: 32 (over z, core), tile: 16 (over y, x).
Axes of the slice: x: 4, y: 4, z: 16, core: 2. Of those that a mesh axis runs over, the one named last changes fastest.
Arguments:
- tile_rows: int32 [32, 1024], P('tm', 'tile'), may hold values from 0 to 31
- tile_cols: int32 [32, 1024], P('tm', 'tile'), may hold values from 0 to 7
- live_tiles: int32 [32, 16], P('tm', 'tile'), may hold values from 32 to 64, as said below
- factor_tiles: bfloat16 [32, 1024, 128, 128], P('tm', 'tile'), may hold values from -0.09375 to 0.09375
- bus_inverse: bfloat16 [32, 128, 128, 128], P('tm', 'tile'), may hold values from -0.5 to 0.5
- bus_coupling: bfloat16 [32, 128, 128, 128], P('tm', 'tile'), may hold values from -0.5 to 0.5
- bus_rhs: bfloat16 [32, 128, 64, 128], P('tm', 'tile'), may hold values from -6 to 6
- row_inverse: bfloat16 [32, 32, 128, 128], P('tm', 'tile'), may hold values from -0.5 to 0.5
- row_rhs: bfloat16 [32, 32, 64, 128], P('tm', 'tile'), may hold values from -6 to 6
- coupling_inverse: float32 [32, 128, 128], P('tm')
- coupling_next: float32 [32, 128, 128], P('tm')
- coupling_rhs: float32 [32, 64, 128], P('tm'), may hold values from -6 to 6
Outputs:
- multipliers: float32 [32, 64, 128], P('tm')
- bus_values: bfloat16 [32, 128, 64, 128], P('tm', 'tile')
- row_values: float32 [32, 32, 64, 128], P('tm', 'tile')
Inputs may be any that keep to these rules, and one draw needn't show every extreme that they name: `live_tiles`: at least one device uses all 64 of its slots.
All inputs are finite; a program needn't handle non-finite values.
Results may differ from a plain program's by a relative error of at most 0.006.
Values sent between devices are 32-bit elements; how exact they have to be, the bound alone decides.
No kernel may reach another device: no remote copies, remote signals or barrier semaphores. Data moves between devices by JAX's collectives and lax.ppermute only.
A program may use at most 64 MiB of HBM per device.

v0:
```python
import jax
import jax.numpy as jnp
from jax import lax
from jax.sharding import PartitionSpec as P

HIGH = lax.Precision.HIGHEST


def passed_along(x, axis, by):
    size = lax.axis_size(axis)
    pairs = [(i, i + by) for i in range(size) if 0 <= i + by < size]
    return lax.ppermute(x, axis, pairs)


def per_device(
    tile_rows,
    tile_cols,
    live_tiles,
    factor_tiles,
    bus_inverse,
    bus_coupling,
    bus_rhs,
    row_inverse,
    row_rhs,
    coupling_inverse,
    coupling_next,
    coupling_rhs,
):
    inverse = coupling_inverse[0]
    nextmat = coupling_next[0]
    rhside = coupling_rhs[0]
    start_zero = jnp.zeros(rhside.shape, jnp.float32)

    def sweep(sweep_index, current):
        beyond = passed_along(current, "tm", -1)
        return jnp.dot(rhside - jnp.dot(beyond, nextmat, precision=HIGH), inverse, precision=HIGH)

    multipliers = lax.fori_loop(0, lax.axis_size("tm"), sweep, start_zero)
    rounded = multipliers.astype(jnp.bfloat16)
    coupled = jnp.einsum(
        "rb,jbc->jrc", rounded, bus_coupling[0], preferred_element_type=jnp.float32
    )
    bus_work = (bus_rhs[0].astype(jnp.float32) - coupled).astype(jnp.bfloat16)
    bus_values = jnp.einsum(
        "jrb,jbc->jrc", bus_work, bus_inverse[0], preferred_element_type=jnp.float32
    ).astype(jnp.bfloat16)
    rows = tile_rows[0]
    cols = tile_cols[0]
    slots = rows.shape[0]
    buses_here = bus_values.shape[0]
    select_table = (cols[:, None] == jnp.arange(buses_here)[None, :]).astype(jnp.bfloat16)
    chosen = jnp.einsum(
        "kj,jrb->krb", select_table, bus_values, preferred_element_type=jnp.float32
    ).astype(jnp.bfloat16)
    live_mask = (jnp.arange(slots) < live_tiles[0, 0]).astype(jnp.float32)
    products = jnp.einsum(
        "krb,kbc->krc", chosen, factor_tiles[0], preferred_element_type=jnp.float32
    )
    products = products * live_mask[:, None, None]
    owned = row_rhs.shape[1]
    total_rows = owned * lax.axis_size("tile")
    onehot = (rows[:, None] == jnp.arange(total_rows)[None, :]).astype(jnp.float32)
    whole = jnp.einsum("ki,krc->irc", onehot, products, precision=HIGH)
    summed = lax.psum(whole, "tile")
    partials = lax.dynamic_slice_in_dim(summed, lax.axis_index("tile") * owned, owned, 0)
    row_work = (row_rhs[0].astype(jnp.float32) - partials).astype(jnp.bfloat16)
    row_values = jnp.einsum(
        "irb,ibc->irc", row_work, row_inverse[0], preferred_element_type=jnp.float32
    )
    return (multipliers[None], bus_values[None], row_values[None])


def solution(mesh):
    placed = (
        P("tm", "tile"),
        P("tm", "tile"),
        P("tm", "tile"),
        P("tm", "tile", None, None),
        P("tm", "tile", None, None),
        P("tm", "tile", None, None),
        P("tm", "tile", None, None),
        P("tm", "tile", None, None),
        P("tm", "tile", None, None),
        P("tm", None, None),
        P("tm", None, None),
        P("tm", None, None),
    )
    return jax.shard_map(
        per_device,
        mesh=mesh,
        in_specs=placed,
        out_specs=(P("tm", None, None), P("tm", "tile", None, None), P("tm", "tile", None, None)),
        check_vma=False,
    )
```

profile of v0, /device:TPU:32, one launch (start us, length us, event | category | flops | bytes accessed | tf_op | source)
XLA Modules:
  0.0 416.8 jit_solution(4158306744137098736)
XLA Ops:
  8.0 259.7 %while.10 = (s32[]{:T(128)}, f32[64,128]{1,0:T(8,128)S(1)}, f32[128,128]{1,0:T(8,128)}, f32[64,128]{1,0:T(8,128)}, f32[128,128]{1,0:T(8,128)}, /*index=5*/s32[]{:T(128)}) while((s32[]{:T(128)}, f32[64,128]{1,0:T(8,128)S(1)}, f32[128,128]{1,0:T(8,128)}, f32[64,128]{1,0:T(8,128)}, f32[128,128]{1,0:T(8,128)}, /*index=5*/s32[]{:T(128)}) %tuple.29), condition=%wide.region_1.0_spmd, body=%wide.region_0.0_spmd.sunk | while | flops 25174016 | bytes 426093 | solution.py:38
  8.1 1.9 collective-permute-start
  13.6 6.7 %collective-permute-start = (f32[64,128]{1,0:T(8,128)S(1)}, f32[64,128]{1,0:T(8,128)S(1)}, u32[]{:S(2)}, u32[]{:S(2)}) collective-permute-start(f32[64,128]{1,0:T(8,128)S(1)} %get-tuple-element.79), channel_id=1, source_target_pairs={{16,0},{32,16},{48,32},{64,48},{80,64},{96,80},{112,96},{128,112},... | collective-permute-start | bytes 98312 | tf_op jit(solution)/shard_map/while/body/eval_jaxpr/ppermute | solution.py:12
  24.0 3.7 collective-permute-start
  31.3 3.7 collective-permute-start
  38.7 3.7 collective-permute-start
  46.0 3.7 collective-permute-start
  53.3 3.7 collective-permute-start
  60.6 3.7 collective-permute-start
  67.9 3.7 collective-permute-start
  75.2 3.7 collective-permute-start
  82.5 3.7 collective-permute-start
  89.9 3.7 collective-permute-start
  97.3 3.5 collective-permute-start
  100.8 2.9 collective-permute-done
  105.8 2.3 collective-permute-start
  108.1 4.1 collective-permute-done
  114.4 1.9 collective-permute-start
  116.3 4.5 %collective-permute-done = f32[64,128]{1,0:T(8,128)S(1)} collective-permute-done((f32[64,128]{1,0:T(8,128)S(1)}, f32[64,128]{1,0:T(8,128)S(1)}, u32[]{:S(2)}, u32[]{:S(2)}) %collective-permute-start) | collective-permute-done | bytes 32800 | tf_op jit(solution)/shard_map/while/body/eval_jaxpr/ppermute | solution.py:12
  122.9 1.9 collective-permute-start
  124.8 4.5 %collective-permute-done = f32[64,128]{1,0:T(8,128)S(1)} collective-permute-done((f32[64,128]{1,0:T(8,128)S(1)}, f32[64,128]{1,0:T(8,128)S(1)}, u32[]{:S(2)}, u32[]{:S(2)}) %collective-permute-start) | collective-permute-done | bytes 32800 | tf_op jit(solution)/shard_map/while/body/eval_jaxpr/ppermute | solution.py:12
  131.4 1.9 collective-permute-start
  133.3 4.5 %collective-permute-done = f32[64,128]{1,0:T(8,128)S(1)} collective-permute-done((f32[64,128]{1,0:T(8,128)S(1)}, f32[64,128]{1,0:T(8,128)S(1)}, u32[]{:S(2)}, u32[]{:S(2)}) %collective-permute-start) | collective-permute-done | bytes 32800 | tf_op jit(solution)/shard_map/while/body/eval_jaxpr/ppermute | solution.py:12
  139.9 1.9 collective-permute-start
  141.9 4.5 %collective-permute-done = f32[64,128]{1,0:T(8,128)S(1)} collective-permute-done((f32[64,128]{1,0:T(8,128)S(1)}, f32[64,128]{1,0:T(8,128)S(1)}, u32[]{:S(2)}, u32[]{:S(2)}) %collective-permute-start) | collective-permute-done | bytes 32800 | tf_op jit(solution)/shard_map/while/body/eval_jaxpr/ppermute | solution.py:12
  148.5 1.9 collective-permute-start
  150.4 4.5 %collective-permute-done = f32[64,128]{1,0:T(8,128)S(1)} collective-permute-done((f32[64,128]{1,0:T(8,128)S(1)}, f32[64,128]{1,0:T(8,128)S(1)}, u32[]{:S(2)}, u32[]{:S(2)}) %collective-permute-start) | collective-permute-done | bytes 32800 | tf_op jit(solution)/shard_map/while/body/eval_jaxpr/ppermute | solution.py:12
  157.0 1.9 collective-permute-start
  158.9 4.5 %collective-permute-done = f32[64,128]{1,0:T(8,128)S(1)} collective-permute-done((f32[64,128]{1,0:T(8,128)S(1)}, f32[64,128]{1,0:T(8,128)S(1)}, u32[]{:S(2)}, u32[]{:S(2)}) %collective-permute-start) | collective-permute-done | bytes 32800 | tf_op jit(solution)/shard_map/while/body/eval_jaxpr/ppermute | solution.py:12
  165.5 1.9 collective-permute-start
  167.4 4.5 %collective-permute-done = f32[64,128]{1,0:T(8,128)S(1)} collective-permute-done((f32[64,128]{1,0:T(8,128)S(1)}, f32[64,128]{1,0:T(8,128)S(1)}, u32[]{:S(2)}, u32[]{:S(2)}) %collective-permute-start) | collective-permute-done | bytes 32800 | tf_op jit(solution)/shard_map/while/body/eval_jaxpr/ppermute | solution.py:12
  174.0 1.9 collective-permute-start
  176.0 4.5 %collective-permute-done = f32[64,128]{1,0:T(8,128)S(1)} collective-permute-done((f32[64,128]{1,0:T(8,128)S(1)}, f32[64,128]{1,0:T(8,128)S(1)}, u32[]{:S(2)}, u32[]{:S(2)}) %collective-permute-start) | collective-permute-done | bytes 32800 | tf_op jit(solution)/shard_map/while/body/eval_jaxpr/ppermute | solution.py:12
  182.6 1.9 collective-permute-start
  184.5 4.5 %collective-permute-done = f32[64,128]{1,0:T(8,128)S(1)} collective-permute-done((f32[64,128]{1,0:T(8,128)S(1)}, f32[64,128]{1,0:T(8,128)S(1)}, u32[]{:S(2)}, u32[]{:S(2)}) %collective-permute-start) | collective-permute-done | bytes 32800 | tf_op jit(solution)/shard_map/while/body/eval_jaxpr/ppermute | solution.py:12
  193.0 4.5 %collective-permute-done = f32[64,128]{1,0:T(8,128)S(1)} collective-permute-done((f32[64,128]{1,0:T(8,128)S(1)}, f32[64,128]{1,0:T(8,128)S(1)}, u32[]{:S(2)}, u32[]{:S(2)}) %collective-permute-start) | collective-permute-done | bytes 32800 | tf_op jit(solution)/shard_map/while/body/eval_jaxpr/ppermute | solution.py:12
  201.5 4.5 %collective-permute-done = f32[64,128]{1,0:T(8,128)S(1)} collective-permute-done((f32[64,128]{1,0:T(8,128)S(1)}, f32[64,128]{1,0:T(8,128)S(1)}, u32[]{:S(2)}, u32[]{:S(2)}) %collective-permute-start) | collective-permute-done | bytes 32800 | tf_op jit(solution)/shard_map/while/body/eval_jaxpr/ppermute | solution.py:12
  210.1 4.5 %collective-permute-done = f32[64,128]{1,0:T(8,128)S(1)} collective-permute-done((f32[64,128]{1,0:T(8,128)S(1)}, f32[64,128]{1,0:T(8,128)S(1)}, u32[]{:S(2)}, u32[]{:S(2)}) %collective-permute-start) | collective-permute-done | bytes 32800 | tf_op jit(solution)/shard_map/while/body/eval_jaxpr/ppermute | solution.py:12
  218.6 4.5 %collective-permute-done = f32[64,128]{1,0:T(8,128)S(1)} collective-permute-done((f32[64,128]{1,0:T(8,128)S(1)}, f32[64,128]{1,0:T(8,128)S(1)}, u32[]{:S(2)}, u32[]{:S(2)}) %collective-permute-start) | collective-permute-done | bytes 32800 | tf_op jit(solution)/shard_map/while/body/eval_jaxpr/ppermute | solution.py:12
  227.1 4.5 %collective-permute-done = f32[64,128]{1,0:T(8,128)S(1)} collective-permute-done((f32[64,128]{1,0:T(8,128)S(1)}, f32[64,128]{1,0:T(8,128)S(1)}, u32[]{:S(2)}, u32[]{:S(2)}) %collective-permute-start) | collective-permute-done | bytes 32800 | tf_op jit(solution)/shard_map/while/body/eval_jaxpr/ppermute | solution.py:12
  235.6 4.5 %collective-permute-done = f32[64,128]{1,0:T(8,128)S(1)} collective-permute-done((f32[64,128]{1,0:T(8,128)S(1)}, f32[64,128]{1,0:T(8,128)S(1)}, u32[]{:S(2)}, u32[]{:S(2)}) %collective-permute-start) | collective-permute-done | bytes 32800 | tf_op jit(solution)/shard_map/while/body/eval_jaxpr/ppermute | solution.py:12
  244.2 4.5 %collective-permute-done = f32[64,128]{1,0:T(8,128)S(1)} collective-permute-done((f32[64,128]{1,0:T(8,128)S(1)}, f32[64,128]{1,0:T(8,128)S(1)}, u32[]{:S(2)}, u32[]{:S(2)}) %collective-permute-start) | collective-permute-done | bytes 32800 | tf_op jit(solution)/shard_map/while/body/eval_jaxpr/ppermute | solution.py:12
  250.7 1.9 collective-permute-start
  252.7 4.5 %collective-permute-done = f32[64,128]{1,0:T(8,128)S(1)} collective-permute-done((f32[64,128]{1,0:T(8,128)S(1)}, f32[64,128]{1,0:T(8,128)S(1)}, u32[]{:S(2)}, u32[]{:S(2)}) %collective-permute-start) | collective-permute-done | bytes 32800 | tf_op jit(solution)/shard_map/while/body/eval_jaxpr/ppermute | solution.py:12
  259.3 1.9 collective-permute-start
  261.2 4.5 %collective-permute-done = f32[64,128]{1,0:T(8,128)S(1)} collective-permute-done((f32[64,128]{1,0:T(8,128)S(1)}, f32[64,128]{1,0:T(8,128)S(1)}, u32[]{:S(2)}, u32[]{:S(2)}) %collective-permute-start) | collective-permute-done | bytes 32800 | tf_op jit(solution)/shard_map/while/body/eval_jaxpr/ppermute | solution.py:12
  271.0 2.1 fusion.2
  274.8 133.6 %all-reduce.2.cloned.1.call-done = f32[32,64,128]{2,1,0:T(8,128)} async-done(((f32[32,64,128]{2,1,0:T(8,128)}), f32[32,64,128]{2,1,0:T(8,128)}) %all-reduce.2.cloned.1.call-update) | async-done | bytes 1048592 | tf_op jit(solution)/shard_map/psum | solution.py:64
  (106 shorter events, 104.5 us)
Async XLA Ops:
  7.2 262.6 %copy-start = (bf16[1,64,128,128]{3,2,1,0:T(8,128)(2,1)S(1)}, bf16[1,64,128,128]{3,2,1,0:T(8,128)(2,1)}, u32[]{:S(2)}) copy-start(bf16[1,64,128,128]{3,2,1,0:T(8,128)(2,1)} %param.17) | copy-start | bytes 6291460
  7.2 262.1 %copy-start.5 = (s32[1,64]{1,0:T(1,128)S(1)}, s32[1,64]{1,0:T(1,128)}, u32[]{:S(2)}) copy-start(s32[1,64]{1,0:T(1,128)} %param.15) | copy-start | bytes 772
  7.2 401.2 %all-reduce.2.cloned.1.call-start = ((), (), s32[]{:S(2)}) async-start(), calls=%async_computation | async-start | bytes 2097152 | tf_op jit(solution)/shard_map/psum | solution.py:64
  8.1 3.5 collective-permute-start
  13.6 8.3 %collective-permute-start = (f32[64,128]{1,0:T(8,128)S(1)}, f32[64,128]{1,0:T(8,128)S(1)}, u32[]{:S(2)}, u32[]{:S(2)}) collective-permute-start(f32[64,128]{1,0:T(8,128)S(1)} %get-tuple-element.79), channel_id=1, source_target_pairs={{16,0},{32,16},{48,32},{64,48},{80,64},{96,80},{112,96},{128,112},... | collective-permute-start | bytes 98312 | tf_op jit(solution)/shard_map/while/body/eval_jaxpr/ppermute | solution.py:12
  24.0 5.2 %collective-permute-start = (f32[64,128]{1,0:T(8,128)S(1)}, f32[64,128]{1,0:T(8,128)S(1)}, u32[]{:S(2)}, u32[]{:S(2)}) collective-permute-start(f32[64,128]{1,0:T(8,128)S(1)} %get-tuple-element.79), channel_id=1, source_target_pairs={{16,0},{32,16},{48,32},{64,48},{80,64},{96,80},{112,96},{128,112},... | collective-permute-start | bytes 98312 | tf_op jit(solution)/shard_map/while/body/eval_jaxpr/ppermute | solution.py:12
  31.3 5.2 %collective-permute-start = (f32[64,128]{1,0:T(8,128)S(1)}, f32[64,128]{1,0:T(8,128)S(1)}, u32[]{:S(2)}, u32[]{:S(2)}) collective-permute-start(f32[64,128]{1,0:T(8,128)S(1)} %get-tuple-element.79), channel_id=1, source_target_pairs={{16,0},{32,16},{48,32},{64,48},{80,64},{96,80},{112,96},{128,112},... | collective-permute-start | bytes 98312 | tf_op jit(solution)/shard_map/while/body/eval_jaxpr/ppermute | solution.py:12
  38.7 5.2 %collective-permute-start = (f32[64,128]{1,0:T(8,128)S(1)}, f32[64,128]{1,0:T(8,128)S(1)}, u32[]{:S(2)}, u32[]{:S(2)}) collective-permute-start(f32[64,128]{1,0:T(8,128)S(1)} %get-tuple-element.79), channel_id=1, source_target_pairs={{16,0},{32,16},{48,32},{64,48},{80,64},{96,80},{112,96},{128,112},... | collective-permute-start | bytes 98312 | tf_op jit(solution)/shard_map/while/body/eval_jaxpr/ppermute | solution.py:12
  46.0 5.2 %collective-permute-start = (f32[64,128]{1,0:T(8,128)S(1)}, f32[64,128]{1,0:T(8,128)S(1)}, u32[]{:S(2)}, u32[]{:S(2)}) collective-permute-start(f32[64,128]{1,0:T(8,128)S(1)} %get-tuple-element.79), channel_id=1, source_target_pairs={{16,0},{32,16},{48,32},{64,48},{80,64},{96,80},{112,96},{128,112},... | collective-permute-start | bytes 98312 | tf_op jit(solution)/shard_map/while/body/eval_jaxpr/ppermute | solution.py:12
  53.3 5.2 %collective-permute-start = (f32[64,128]{1,0:T(8,128)S(1)}, f32[64,128]{1,0:T(8,128)S(1)}, u32[]{:S(2)}, u32[]{:S(2)}) collective-permute-start(f32[64,128]{1,0:T(8,128)S(1)} %get-tuple-element.79), channel_id=1, source_target_pairs={{16,0},{32,16},{48,32},{64,48},{80,64},{96,80},{112,96},{128,112},... | collective-permute-start | bytes 98312 | tf_op jit(solution)/shard_map/while/body/eval_jaxpr/ppermute | solution.py:12
  60.6 5.2 %collective-permute-start = (f32[64,128]{1,0:T(8,128)S(1)}, f32[64,128]{1,0:T(8,128)S(1)}, u32[]{:S(2)}, u32[]{:S(2)}) collective-permute-start(f32[64,128]{1,0:T(8,128)S(1)} %get-tuple-element.79), channel_id=1, source_target_pairs={{16,0},{32,16},{48,32},{64,48},{80,64},{96,80},{112,96},{128,112},... | collective-permute-start | bytes 98312 | tf_op jit(solution)/shard_map/while/body/eval_jaxpr/ppermute | solution.py:12
  67.9 5.2 %collective-permute-start = (f32[64,128]{1,0:T(8,128)S(1)}, f32[64,128]{1,0:T(8,128)S(1)}, u32[]{:S(2)}, u32[]{:S(2)}) collective-permute-start(f32[64,128]{1,0:T(8,128)S(1)} %get-tuple-element.79), channel_id=1, source_target_pairs={{16,0},{32,16},{48,32},{64,48},{80,64},{96,80},{112,96},{128,112},... | collective-permute-start | bytes 98312 | tf_op jit(solution)/shard_map/while/body/eval_jaxpr/ppermute | solution.py:12
  75.2 5.2 %collective-permute-start = (f32[64,128]{1,0:T(8,128)S(1)}, f32[64,128]{1,0:T(8,128)S(1)}, u32[]{:S(2)}, u32[]{:S(2)}) collective-permute-start(f32[64,128]{1,0:T(8,128)S(1)} %get-tuple-element.79), channel_id=1, source_target_pairs={{16,0},{32,16},{48,32},{64,48},{80,64},{96,80},{112,96},{128,112},... | collective-permute-start | bytes 98312 | tf_op jit(solution)/shard_map/while/body/eval_jaxpr/ppermute | solution.py:12
  82.5 5.2 %collective-permute-start = (f32[64,128]{1,0:T(8,128)S(1)}, f32[64,128]{1,0:T(8,128)S(1)}, u32[]{:S(2)}, u32[]{:S(2)}) collective-permute-start(f32[64,128]{1,0:T(8,128)S(1)} %get-tuple-element.79), channel_id=1, source_target_pairs={{16,0},{32,16},{48,32},{64,48},{80,64},{96,80},{112,96},{128,112},... | collective-permute-start | bytes 98312 | tf_op jit(solution)/shard_map/while/body/eval_jaxpr/ppermute | solution.py:12
  89.9 5.4 %collective-permute-start = (f32[64,128]{1,0:T(8,128)S(1)}, f32[64,128]{1,0:T(8,128)S(1)}, u32[]{:S(2)}, u32[]{:S(2)}) collective-permute-start(f32[64,128]{1,0:T(8,128)S(1)} %get-tuple-element.79), channel_id=1, source_target_pairs={{16,0},{32,16},{48,32},{64,48},{80,64},{96,80},{112,96},{128,112},... | collective-permute-start | bytes 98312 | tf_op jit(solution)/shard_map/while/body/eval_jaxpr/ppermute | solution.py:12
  97.3 6.4 %collective-permute-start = (f32[64,128]{1,0:T(8,128)S(1)}, f32[64,128]{1,0:T(8,128)S(1)}, u32[]{:S(2)}, u32[]{:S(2)}) collective-permute-start(f32[64,128]{1,0:T(8,128)S(1)} %get-tuple-element.79), channel_id=1, source_target_pairs={{16,0},{32,16},{48,32},{64,48},{80,64},{96,80},{112,96},{128,112},... | collective-permute-start | bytes 98312 | tf_op jit(solution)/shard_map/while/body/eval_jaxpr/ppermute | solution.py:12
  105.8 6.4 %collective-permute-start = (f32[64,128]{1,0:T(8,128)S(1)}, f32[64,128]{1,0:T(8,128)S(1)}, u32[]{:S(2)}, u32[]{:S(2)}) collective-permute-start(f32[64,128]{1,0:T(8,128)S(1)} %get-tuple-element.79), channel_id=1, source_target_pairs={{16,0},{32,16},{48,32},{64,48},{80,64},{96,80},{112,96},{128,112},... | collective-permute-start | bytes 98312 | tf_op jit(solution)/shard_map/while/body/eval_jaxpr/ppermute | solution.py:12
  114.4 6.4 %collective-permute-start = (f32[64,128]{1,0:T(8,128)S(1)}, f32[64,128]{1,0:T(8,128)S(1)}, u32[]{:S(2)}, u32[]{:S(2)}) collective-permute-start(f32[64,128]{1,0:T(8,128)S(1)} %get-tuple-element.79), channel_id=1, source_target_pairs={{16,0},{32,16},{48,32},{64,48},{80,64},{96,80},{112,96},{128,112},... | collective-permute-start | bytes 98312 | tf_op jit(solution)/shard_map/while/body/eval_jaxpr/ppermute | solution.py:12
  122.9 6.4 %collective-permute-start = (f32[64,128]{1,0:T(8,128)S(1)}, f32[64,128]{1,0:T(8,128)S(1)}, u32[]{:S(2)}, u32[]{:S(2)}) collective-permute-start(f32[64,128]{1,0:T(8,128)S(1)} %get-tuple-element.79), channel_id=1, source_target_pairs={{16,0},{32,16},{48,32},{64,48},{80,64},{96,80},{112,96},{128,112},... | collective-permute-start | bytes 98312 | tf_op jit(solution)/shard_map/while/body/eval_jaxpr/ppermute | solution.py:12
  131.4 6.4 %collective-permute-start = (f32[64,128]{1,0:T(8,128)S(1)}, f32[64,128]{1,0:T(8,128)S(1)}, u32[]{:S(2)}, u32[]{:S(2)}) collective-permute-start(f32[64,128]{1,0:T(8,128)S(1)} %get-tuple-element.79), channel_id=1, source_target_pairs={{16,0},{32,16},{48,32},{64,48},{80,64},{96,80},{112,96},{128,112},... | collective-permute-start | bytes 98312 | tf_op jit(solution)/shard_map/while/body/eval_jaxpr/ppermute | solution.py:12
  139.9 6.4 %collective-permute-start = (f32[64,128]{1,0:T(8,128)S(1)}, f32[64,128]{1,0:T(8,128)S(1)}, u32[]{:S(2)}, u32[]{:S(2)}) collective-permute-start(f32[64,128]{1,0:T(8,128)S(1)} %get-tuple-element.79), channel_id=1, source_target_pairs={{16,0},{32,16},{48,32},{64,48},{80,64},{96,80},{112,96},{128,112},... | collective-permute-start | bytes 98312 | tf_op jit(solution)/shard_map/while/body/eval_jaxpr/ppermute | solution.py:12
  148.5 6.4 %collective-permute-start = (f32[64,128]{1,0:T(8,128)S(1)}, f32[64,128]{1,0:T(8,128)S(1)}, u32[]{:S(2)}, u32[]{:S(2)}) collective-permute-start(f32[64,128]{1,0:T(8,128)S(1)} %get-tuple-element.79), channel_id=1, source_target_pairs={{16,0},{32,16},{48,32},{64,48},{80,64},{96,80},{112,96},{128,112},... | collective-permute-start | bytes 98312 | tf_op jit(solution)/shard_map/while/body/eval_jaxpr/ppermute | solution.py:12
  157.0 6.4 %collective-permute-start = (f32[64,128]{1,0:T(8,128)S(1)}, f32[64,128]{1,0:T(8,128)S(1)}, u32[]{:S(2)}, u32[]{:S(2)}) collective-permute-start(f32[64,128]{1,0:T(8,128)S(1)} %get-tuple-element.79), channel_id=1, source_target_pairs={{16,0},{32,16},{48,32},{64,48},{80,64},{96,80},{112,96},{128,112},... | collective-permute-start | bytes 98312 | tf_op jit(solution)/shard_map/while/body/eval_jaxpr/ppermute | solution.py:12
  165.5 6.4 %collective-permute-start = (f32[64,128]{1,0:T(8,128)S(1)}, f32[64,128]{1,0:T(8,128)S(1)}, u32[]{:S(2)}, u32[]{:S(2)}) collective-permute-start(f32[64,128]{1,0:T(8,128)S(1)} %get-tuple-element.79), channel_id=1, source_target_pairs={{16,0},{32,16},{48,32},{64,48},{80,64},{96,80},{112,96},{128,112},... | collective-permute-start | bytes 98312 | tf_op jit(solution)/shard_map/while/body/eval_jaxpr/ppermute | solution.py:12
  174.0 6.4 %collective-permute-start = (f32[64,128]{1,0:T(8,128)S(1)}, f32[64,128]{1,0:T(8,128)S(1)}, u32[]{:S(2)}, u32[]{:S(2)}) collective-permute-start(f32[64,128]{1,0:T(8,128)S(1)} %get-tuple-element.79), channel_id=1, source_target_pairs={{16,0},{32,16},{48,32},{64,48},{80,64},{96,80},{112,96},{128,112},... | collective-permute-start | bytes 98312 | tf_op jit(solution)/shard_map/while/body/eval_jaxpr/ppermute | solution.py:12
  182.6 6.4 %collective-permute-start = (f32[64,128]{1,0:T(8,128)S(1)}, f32[64,128]{1,0:T(8,128)S(1)}, u32[]{:S(2)}, u32[]{:S(2)}) collective-permute-start(f32[64,128]{1,0:T(8,128)S(1)} %get-tuple-element.79), channel_id=1, source_target_pairs={{16,0},{32,16},{48,32},{64,48},{80,64},{96,80},{112,96},{128,112},... | collective-permute-start | bytes 98312 | tf_op jit(solution)/shard_map/while/body/eval_jaxpr/ppermute | solution.py:12
  191.1 6.4 %collective-permute-start = (f32[64,128]{1,0:T(8,128)S(1)}, f32[64,128]{1,0:T(8,128)S(1)}, u32[]{:S(2)}, u32[]{:S(2)}) collective-permute-start(f32[64,128]{1,0:T(8,128)S(1)} %get-tuple-element.79), channel_id=1, source_target_pairs={{16,0},{32,16},{48,32},{64,48},{80,64},{96,80},{112,96},{128,112},... | collective-permute-start | bytes 98312 | tf_op jit(solution)/shard_map/while/body/eval_jaxpr/ppermute | solution.py:12
  199.6 6.4 %collective-permute-start = (f32[64,128]{1,0:T(8,128)S(1)}, f32[64,128]{1,0:T(8,128)S(1)}, u32[]{:S(2)}, u32[]{:S(2)}) collective-permute-start(f32[64,128]{1,0:T(8,128)S(1)} %get-tuple-element.79), channel_id=1, source_target_pairs={{16,0},{32,16},{48,32},{64,48},{80,64},{96,80},{112,96},{128,112},... | collective-permute-start | bytes 98312 | tf_op jit(solution)/shard_map/while/body/eval_jaxpr/ppermute | solution.py:12
  208.1 6.4 %collective-permute-start = (f32[64,128]{1,0:T(8,128)S(1)}, f32[64,128]{1,0:T(8,128)S(1)}, u32[]{:S(2)}, u32[]{:S(2)}) collective-permute-start(f32[64,128]{1,0:T(8,128)S(1)} %get-tuple-element.79), channel_id=1, source_target_pairs={{16,0},{32,16},{48,32},{64,48},{80,64},{96,80},{112,96},{128,112},... | collective-permute-start | bytes 98312 | tf_op jit(solution)/shard_map/while/body/eval_jaxpr/ppermute | solution.py:12
  216.6 6.4 %collective-permute-start = (f32[64,128]{1,0:T(8,128)S(1)}, f32[64,128]{1,0:T(8,128)S(1)}, u32[]{:S(2)}, u32[]{:S(2)}) collective-permute-start(f32[64,128]{1,0:T(8,128)S(1)} %get-tuple-element.79), channel_id=1, source_target_pairs={{16,0},{32,16},{48,32},{64,48},{80,64},{96,80},{112,96},{128,112},... | collective-permute-start | bytes 98312 | tf_op jit(solution)/shard_map/while/body/eval_jaxpr/ppermute | solution.py:12
  225.2 6.4 %collective-permute-start = (f32[64,128]{1,0:T(8,128)S(1)}, f32[64,128]{1,0:T(8,128)S(1)}, u32[]{:S(2)}, u32[]{:S(2)}) collective-permute-start(f32[64,128]{1,0:T(8,128)S(1)} %get-tuple-element.79), channel_id=1, source_target_pairs={{16,0},{32,16},{48,32},{64,48},{80,64},{96,80},{112,96},{128,112},... | collective-permute-start | bytes 98312 | tf_op jit(solution)/shard_map/while/body/eval_jaxpr/ppermute | solution.py:12
  233.7 6.4 %collective-permute-start = (f32[64,128]{1,0:T(8,128)S(1)}, f32[64,128]{1,0:T(8,128)S(1)}, u32[]{:S(2)}, u32[]{:S(2)}) collective-permute-start(f32[64,128]{1,0:T(8,128)S(1)} %get-tuple-element.79), channel_id=1, source_target_pairs={{16,0},{32,16},{48,32},{64,48},{80,64},{96,80},{112,96},{128,112},... | collective-permute-start | bytes 98312 | tf_op jit(solution)/shard_map/while/body/eval_jaxpr/ppermute | solution.py:12
  242.2 6.4 %collective-permute-start = (f32[64,128]{1,0:T(8,128)S(1)}, f32[64,128]{1,0:T(8,128)S(1)}, u32[]{:S(2)}, u32[]{:S(2)}) collective-permute-start(f32[64,128]{1,0:T(8,128)S(1)} %get-tuple-element.79), channel_id=1, source_target_pairs={{16,0},{32,16},{48,32},{64,48},{80,64},{96,80},{112,96},{128,112},... | collective-permute-start | bytes 98312 | tf_op jit(solution)/shard_map/while/body/eval_jaxpr/ppermute | solution.py:12
  250.7 6.4 %collective-permute-start = (f32[64,128]{1,0:T(8,128)S(1)}, f32[64,128]{1,0:T(8,128)S(1)}, u32[]{:S(2)}, u32[]{:S(2)}) collective-permute-start(f32[64,128]{1,0:T(8,128)S(1)} %get-tuple-element.79), channel_id=1, source_target_pairs={{16,0},{32,16},{48,32},{64,48},{80,64},{96,80},{112,96},{128,112},... | collective-permute-start | bytes 98312 | tf_op jit(solution)/shard_map/while/body/eval_jaxpr/ppermute | solution.py:12
  259.3 6.4 %collective-permute-start = (f32[64,128]{1,0:T(8,128)S(1)}, f32[64,128]{1,0:T(8,128)S(1)}, u32[]{:S(2)}, u32[]{:S(2)}) collective-permute-start(f32[64,128]{1,0:T(8,128)S(1)} %get-tuple-element.79), channel_id=1, source_target_pairs={{16,0},{32,16},{48,32},{64,48},{80,64},{96,80},{112,96},{128,112},... | collective-permute-start | bytes 98312 | tf_op jit(solution)/shard_map/while/body/eval_jaxpr/ppermute | solution.py:12
  267.8 3.2 copy-start.2
  269.2 1.8 copy-start.1
  269.8 1.2 copy-start.6
  273.1 135.3 %copy-start.3 = (bf16[1,2,128,128]{3,2,1,0:T(8,128)(2,1)S(1)}, bf16[1,2,128,128]{3,2,1,0:T(8,128)(2,1)}, u32[]{:S(2)}) copy-start(bf16[1,2,128,128]{3,2,1,0:T(8,128)(2,1)} %param.21) | copy-start | bytes 196612
  273.1 135.3 %copy-start.4 = (bf16[1,2,64,128]{3,2,1,0:T(8,128)(2,1)S(1)}, bf16[1,2,64,128]{3,2,1,0:T(8,128)(2,1)}, u32[]{:S(2)}) copy-start(bf16[1,2,64,128]{3,2,1,0:T(8,128)(2,1)} %param.22) | copy-start | bytes 98308
Sparse Core Ops, SparseCore 0:
  274.9 133.4 all-reduce.1
where the time goes:
time: 421 us; the launch traced here: 417 us
  waiting for transfers between devices  241 us (57%)
  starting transfers between devices  85.6 us (20%)
  matrix products  72.4 us (17%)
  between operations  15 us (4%)
    psum x1, waiting for transfers between devices, per_device(): summed = lax.psum(whole, 'tile')  134 us
    ppermute x32, waiting for transfers between devices, passed_along(): return lax.ppermute(x, axis, pairs)  107 us
    ppermute x32, starting transfers between devices, passed_along(): return lax.ppermute(x, axis, pairs)  85.5 us
    dot_general x32, matrix products, sweep(): jnp.dot(rhside - jnp.dot(beyond, nextmat, precision=HIGH), inverse, preci...  32.8 us
    dot_general x32, matrix products, sweep(): jnp.dot(beyond, nextmat, precision=HIGH)  32.8 us
  transfers between devices with their start and end apart: 33, of which 33 were waited for; matrix products, arithmetic and copies ran while one was open for 0% of the time, Pallas kernels for 0%

commit v1 on v0

--- a/solution.py
+++ b/solution.py
@@ -61,7 +61,9 @@
     total_rows = owned * lax.axis_size("tile")
     onehot = (rows[:, None] == jnp.arange(total_rows)[None, :]).astype(jnp.float32)
     whole = jnp.einsum("ki,krc->irc", onehot, products, precision=HIGH)
-    summed = lax.psum(whole, "tile")
+    summed = whole
+    for hop in (1, 2, 4, 8):
+        summed = summed + lax.ppermute(summed, "tile", [(dev, dev ^ hop) for dev in range(16)])
     partials = lax.dynamic_slice_in_dim(summed, lax.axis_index("tile") * owned, owned, 0)
     row_work = (row_rhs[0].astype(jnp.float32) - partials).astype(jnp.bfloat16)
     row_values = jnp.einsum(

time: 421 us -> 392 us (0.931)
  the two profiles are of different devices: /device:TPU:32 before, /device:TPU:238 now
where the time goes in v1:
time: 392 us; the launch traced here: 388 us
  waiting for transfers between devices  235 us (60%)
  starting transfers between devices  77 us (20%)
  matrix products  71.6 us (18%)
    ppermute x32, waiting for transfers between devices, passed_along(): return lax.ppermute(x, axis, pairs)  138 us
    ppermute x4, waiting for transfers between devices, per_device(): lax.ppermute(summed, 'tile', [(dev, dev ^ hop) for dev in range(16)])  96.5 us
    ppermute x32, starting transfers between devices, passed_along(): return lax.ppermute(x, axis, pairs)  64.3 us
    dot_general x32, matrix products, sweep(): jnp.dot(rhside - jnp.dot(beyond, nextmat, precision=HIGH), inverse, preci...  32.8 us
    dot_general x32, matrix products, sweep(): jnp.dot(beyond, nextmat, precision=HIGH)  32.8 us
    ppermute x4, starting transfers between devices, per_device(): lax.ppermute(summed, 'tile', [(dev, dev ^ hop) for dev in range(16)])  12.7 us
  transfers between devices with their start and end apart: 36, of which 36 were waited for; matrix products, arithmetic and copies ran while one was open for 0% of the time, Pallas kernels for 0%

profile of v1, /device:TPU:238, one launch (start us, length us, event | category | flops | bytes accessed | tf_op | source)
XLA Modules:
  0.0 387.8 jit_solution(13061295572931008108)
XLA Ops:
  1.5 269.2 %while.10 = (s32[]{:T(128)}, f32[64,128]{1,0:T(8,128)S(1)}, f32[128,128]{1,0:T(8,128)}, f32[64,128]{1,0:T(8,128)}, f32[128,128]{1,0:T(8,128)}, /*index=5*/s32[]{:T(128)}) while((s32[]{:T(128)}, f32[64,128]{1,0:T(8,128)S(1)}, f32[128,128]{1,0:T(8,128)}, f32[64,128]{1,0:T(8,128)}, f32[128,128]{1,0:T(8,128)}, /*index=5*/s32[]{:T(128)}) %tuple.27), condition=%wide.region_1.0_spmd, body=%wide.region_0.0_spmd.sunk | while | flops 25174016 | bytes 426093 | solution.py:38
  7.1 3.7 collective-permute-start
  10.7 2.2 collective-permute-done
  15.0 3.0 collective-permute-start
  18.1 3.4 collective-permute-done
  25.5 4.5 %collective-permute-done = f32[64,128]{1,0:T(8,128)S(1)} collective-permute-done((f32[64,128]{1,0:T(8,128)S(1)}, f32[64,128]{1,0:T(8,128)S(1)}, u32[]{:S(2)}, u32[]{:S(2)}) %collective-permute-start) | collective-permute-done | bytes 32800 | tf_op jit(solution)/shard_map/while/body/eval_jaxpr/ppermute | solution.py:12
  32.1 1.9 collective-permute-start
  34.0 4.5 %collective-permute-done = f32[64,128]{1,0:T(8,128)S(1)} collective-permute-done((f32[64,128]{1,0:T(8,128)S(1)}, f32[64,128]{1,0:T(8,128)S(1)}, u32[]{:S(2)}, u32[]{:S(2)}) %collective-permute-start) | collective-permute-done | bytes 32800 | tf_op jit(solution)/shard_map/while/body/eval_jaxpr/ppermute | solution.py:12
  42.5 4.5 %collective-permute-done = f32[64,128]{1,0:T(8,128)S(1)} collective-permute-done((f32[64,128]{1,0:T(8,128)S(1)}, f32[64,128]{1,0:T(8,128)S(1)}, u32[]{:S(2)}, u32[]{:S(2)}) %collective-permute-start) | collective-permute-done | bytes 32800 | tf_op jit(solution)/shard_map/while/body/eval_jaxpr/ppermute | solution.py:12
  49.1 1.9 collective-permute-start
  51.0 4.5 %collective-permute-done = f32[64,128]{1,0:T(8,128)S(1)} collective-permute-done((f32[64,128]{1,0:T(8,128)S(1)}, f32[64,128]{1,0:T(8,128)S(1)}, u32[]{:S(2)}, u32[]{:S(2)}) %collective-permute-start) | collective-permute-done | bytes 32800 | tf_op jit(solution)/shard_map/while/body/eval_jaxpr/ppermute | solution.py:12
  59.6 4.5 %collective-permute-done = f32[64,128]{1,0:T(8,128)S(1)} collective-permute-done((f32[64,128]{1,0:T(8,128)S(1)}, f32[64,128]{1,0:T(8,128)S(1)}, u32[]{:S(2)}, u32[]{:S(2)}) %collective-permute-start) | collective-permute-done | bytes 32800 | tf_op jit(solution)/shard_map/while/body/eval_jaxpr/ppermute | solution.py:12
  68.1 4.5 %collective-permute-done = f32[64,128]{1,0:T(8,128)S(1)} collective-permute-done((f32[64,128]{1,0:T(8,128)S(1)}, f32[64,128]{1,0:T(8,128)S(1)}, u32[]{:S(2)}, u32[]{:S(2)}) %collective-permute-start) | collective-permute-done | bytes 32800 | tf_op jit(solution)/shard_map/while/body/eval_jaxpr/ppermute | solution.py:12
  76.6 4.5 %collective-permute-done = f32[64,128]{1,0:T(8,128)S(1)} collective-permute-done((f32[64,128]{1,0:T(8,128)S(1)}, f32[64,128]{1,0:T(8,128)S(1)}, u32[]{:S(2)}, u32[]{:S(2)}) %collective-permute-start) | collective-permute-done | bytes 32800 | tf_op jit(solution)/shard_map/while/body/eval_jaxpr/ppermute | solution.py:12
  85.1 4.5 %collective-permute-done = f32[64,128]{1,0:T(8,128)S(1)} collective-permute-done((f32[64,128]{1,0:T(8,128)S(1)}, f32[64,128]{1,0:T(8,128)S(1)}, u32[]{:S(2)}, u32[]{:S(2)}) %collective-permute-start) | collective-permute-done | bytes 32800 | tf_op jit(solution)/shard_map/while/body/eval_jaxpr/ppermute | solution.py:12
  93.7 4.5 %collective-permute-done = f32[64,128]{1,0:T(8,128)S(1)} collective-permute-done((f32[64,128]{1,0:T(8,128)S(1)}, f32[64,128]{1,0:T(8,128)S(1)}, u32[]{:S(2)}, u32[]{:S(2)}) %collective-permute-start) | collective-permute-done | bytes 32800 | tf_op jit(solution)/shard_map/while/body/eval_jaxpr/ppermute | solution.py:12
  102.2 4.5 %collective-permute-done = f32[64,128]{1,0:T(8,128)S(1)} collective-permute-done((f32[64,128]{1,0:T(8,128)S(1)}, f32[64,128]{1,0:T(8,128)S(1)}, u32[]{:S(2)}, u32[]{:S(2)}) %collective-permute-start) | collective-permute-done | bytes 32800 | tf_op jit(solution)/shard_map/while/body/eval_jaxpr/ppermute | solution.py:12
  110.7 4.5 %collective-permute-done = f32[64,128]{1,0:T(8,128)S(1)} collective-permute-done((f32[64,128]{1,0:T(8,128)S(1)}, f32[64,128]{1,0:T(8,128)S(1)}, u32[]{:S(2)}, u32[]{:S(2)}) %collective-permute-start) | collective-permute-done | bytes 32800 | tf_op jit(solution)/shard_map/while/body/eval_jaxpr/ppermute | solution.py:12
  119.2 4.5 %collective-permute-done = f32[64,128]{1,0:T(8,128)S(1)} collective-permute-done((f32[64,128]{1,0:T(8,128)S(1)}, f32[64,128]{1,0:T(8,128)S(1)}, u32[]{:S(2)}, u32[]{:S(2)}) %collective-permute-start) | collective-permute-done | bytes 32800 | tf_op jit(solution)/shard_map/while/body/eval_jaxpr/ppermute | solution.py:12
  125.8 1.9 collective-permute-start
  127.8 4.5 %collective-permute-done = f32[64,128]{1,0:T(8,128)S(1)} collective-permute-done((f32[64,128]{1,0:T(8,128)S(1)}, f32[64,128]{1,0:T(8,128)S(1)}, u32[]{:S(2)}, u32[]{:S(2)}) %collective-permute-start) | collective-permute-done | bytes 32800 | tf_op jit(solution)/shard_map/while/body/eval_jaxpr/ppermute | solution.py:12
  136.3 4.5 %collective-permute-done = f32[64,128]{1,0:T(8,128)S(1)} collective-permute-done((f32[64,128]{1,0:T(8,128)S(1)}, f32[64,128]{1,0:T(8,128)S(1)}, u32[]{:S(2)}, u32[]{:S(2)}) %collective-permute-start) | collective-permute-done | bytes 32800 | tf_op jit(solution)/shard_map/while/body/eval_jaxpr/ppermute | solution.py:12
  144.8 4.5 %collective-permute-done = f32[64,128]{1,0:T(8,128)S(1)} collective-permute-done((f32[64,128]{1,0:T(8,128)S(1)}, f32[64,128]{1,0:T(8,128)S(1)}, u32[]{:S(2)}, u32[]{:S(2)}) %collective-permute-start) | collective-permute-done | bytes 32800 | tf_op jit(solution)/shard_map/while/body/eval_jaxpr/ppermute | solution.py:12
  153.3 4.5 %collective-permute-done = f32[64,128]{1,0:T(8,128)S(1)} collective-permute-done((f32[64,128]{1,0:T(8,128)S(1)}, f32[64,128]{1,0:T(8,128)S(1)}, u32[]{:S(2)}, u32[]{:S(2)}) %collective-permute-start) | collective-permute-done | bytes 32800 | tf_op jit(solution)/shard_map/while/body/eval_jaxpr/ppermute | solution.py:12
  159.9 1.9 collective-permute-start
  161.9 4.5 %collective-permute-done = f32[64,128]{1,0:T(8,128)S(1)} collective-permute-done((f32[64,128]{1,0:T(8,128)S(1)}, f32[64,128]{1,0:T(8,128)S(1)}, u32[]{:S(2)}, u32[]{:S(2)}) %collective-permute-start) | collective-permute-done | bytes 32800 | tf_op jit(solution)/shard_map/while/body/eval_jaxpr/ppermute | solution.py:12
  170.4 4.5 %collective-permute-done = f32[64,128]{1,0:T(8,128)S(1)} collective-permute-done((f32[64,128]{1,0:T(8,128)S(1)}, f32[64,128]{1,0:T(8,128)S(1)}, u32[]{:S(2)}, u32[]{:S(2)}) %collective-permute-start) | collective-permute-done | bytes 32800 | tf_op jit(solution)/shard_map/while/body/eval_jaxpr/ppermute | solution.py:12
  177.0 1.9 collective-permute-start
  178.9 4.5 %collective-permute-done = f32[64,128]{1,0:T(8,128)S(1)} collective-permute-done((f32[64,128]{1,0:T(8,128)S(1)}, f32[64,128]{1,0:T(8,128)S(1)}, u32[]{:S(2)}, u32[]{:S(2)}) %collective-permute-start) | collective-permute-done | bytes 32800 | tf_op jit(solution)/shard_map/while/body/eval_jaxpr/ppermute | solution.py:12
  187.4 4.5 %collective-permute-done = f32[64,128]{1,0:T(8,128)S(1)} collective-permute-done((f32[64,128]{1,0:T(8,128)S(1)}, f32[64,128]{1,0:T(8,128)S(1)}, u32[]{:S(2)}, u32[]{:S(2)}) %collective-permute-start) | collective-permute-done | bytes 32800 | tf_op jit(solution)/shard_map/while/body/eval_jaxpr/ppermute | solution.py:12
  196.0 4.5 %collective-permute-done = f32[64,128]{1,0:T(8,128)S(1)} collective-permute-done((f32[64,128]{1,0:T(8,128)S(1)}, f32[64,128]{1,0:T(8,128)S(1)}, u32[]{:S(2)}, u32[]{:S(2)}) %collective-permute-start) | collective-permute-done | bytes 32800 | tf_op jit(solution)/shard_map/while/body/eval_jaxpr/ppermute | solution.py:12
  204.5 4.5 %collective-permute-done = f32[64,128]{1,0:T(8,128)S(1)} collective-permute-done((f32[64,128]{1,0:T(8,128)S(1)}, f32[64,128]{1,0:T(8,128)S(1)}, u32[]{:S(2)}, u32[]{:S(2)}) %collective-permute-start) | collective-permute-done | bytes 32800 | tf_op jit(solution)/shard_map/while/body/eval_jaxpr/ppermute | solution.py:12
  213.0 4.5 %collective-permute-done = f32[64,128]{1,0:T(8,128)S(1)} collective-permute-done((f32[64,128]{1,0:T(8,128)S(1)}, f32[64,128]{1,0:T(8,128)S(1)}, u32[]{:S(2)}, u32[]{:S(2)}) %collective-permute-start) | collective-permute-done | bytes 32800 | tf_op jit(solution)/shard_map/while/body/eval_jaxpr/ppermute | solution.py:12
  221.5 4.5 %collective-permute-done = f32[64,128]{1,0:T(8,128)S(1)} collective-permute-done((f32[64,128]{1,0:T(8,128)S(1)}, f32[64,128]{1,0:T(8,128)S(1)}, u32[]{:S(2)}, u32[]{:S(2)}) %collective-permute-start) | collective-permute-done | bytes 32800 | tf_op jit(solution)/shard_map/while/body/eval_jaxpr/ppermute | solution.py:12
  230.1 4.5 %collective-permute-done = f32[64,128]{1,0:T(8,128)S(1)} collective-permute-done((f32[64,128]{1,0:T(8,128)S(1)}, f32[64,128]{1,0:T(8,128)S(1)}, u32[]{:S(2)}, u32[]{:S(2)}) %collective-permute-start) | collective-permute-done | bytes 32800 | tf_op jit(solution)/shard_map/while/body/eval_jaxpr/ppermute | solution.py:12
  238.6 4.5 %collective-permute-done = f32[64,128]{1,0:T(8,128)S(1)} collective-permute-done((f32[64,128]{1,0:T(8,128)S(1)}, f32[64,128]{1,0:T(8,128)S(1)}, u32[]{:S(2)}, u32[]{:S(2)}) %collective-permute-start) | collective-permute-done | bytes 32800 | tf_op jit(solution)/shard_map/while/body/eval_jaxpr/ppermute | solution.py:12
  247.1 4.5 %collective-permute-done = f32[64,128]{1,0:T(8,128)S(1)} collective-permute-done((f32[64,128]{1,0:T(8,128)S(1)}, f32[64,128]{1,0:T(8,128)S(1)}, u32[]{:S(2)}, u32[]{:S(2)}) %collective-permute-start) | collective-permute-done | bytes 32800 | tf_op jit(solution)/shard_map/while/body/eval_jaxpr/ppermute | solution.py:12
  255.6 4.5 %collective-permute-done = f32[64,128]{1,0:T(8,128)S(1)} collective-permute-done((f32[64,128]{1,0:T(8,128)S(1)}, f32[64,128]{1,0:T(8,128)S(1)}, u32[]{:S(2)}, u32[]{:S(2)}) %collective-permute-start) | collective-permute-done | bytes 32800 | tf_op jit(solution)/shard_map/while/body/eval_jaxpr/ppermute | solution.py:12
  264.1 4.5 %collective-permute-done = f32[64,128]{1,0:T(8,128)S(1)} collective-permute-done((f32[64,128]{1,0:T(8,128)S(1)}, f32[64,128]{1,0:T(8,128)S(1)}, u32[]{:S(2)}, u32[]{:S(2)}) %collective-permute-start) | collective-permute-done | bytes 32800 | tf_op jit(solution)/shard_map/while/body/eval_jaxpr/ppermute | solution.py:12
  274.0 2.1 fusion.2
  276.0 2.7 collective-permute-start.1
  278.8 22.3 %collective-permute-done.1 = f32[32,64,128]{2,0,1:T(8,128)S(1)} collective-permute-done((f32[32,64,128]{2,0,1:T(8,128)S(1)}, f32[32,64,128]{2,0,1:T(8,128)S(1)}, u32[]{:S(2)}, u32[]{:S(2)}) %collective-permute-start.1) | collective-permute-done | bytes 1048608 | tf_op jit(solution)/shard_map/ppermute | solution.py:66
  301.3 3.3 collective-permute-start.2
  304.6 24.4 %collective-permute-done.2 = f32[32,64,128]{2,0,1:T(8,128)S(1)} collective-permute-done((f32[32,64,128]{2,0,1:T(8,128)S(1)}, f32[32,64,128]{2,0,1:T(8,128)S(1)}, u32[]{:S(2)}, u32[]{:S(2)}) %collective-permute-start.2) | collective-permute-done | bytes 1048608 | tf_op jit(solution)/shard_map/ppermute | solution.py:66
  329.3 2.5 collective-permute-start.3
  331.8 25.0 %collective-permute-done.3 = f32[32,64,128]{2,0,1:T(8,128)S(1)} collective-permute-done((f32[32,64,128]{2,0,1:T(8,128)S(1)}, f32[32,64,128]{2,0,1:T(8,128)S(1)}, u32[]{:S(2)}, u32[]{:S(2)}) %collective-permute-start.3) | collective-permute-done | bytes 1048608 | tf_op jit(solution)/shard_map/ppermute | solution.py:66
  357.0 4.2 %collective-permute-start.4 = (f32[32,64,128]{2,0,1:T(8,128)S(1)}, f32[32,64,128]{2,0,1:T(8,128)}, u32[]{:S(2)}, u32[]{:S(2)}) collective-permute-start(f32[32,64,128]{2,0,1:T(8,128)S(1)} %add.20), channel_id=1, source_target_pairs={{0,8},{1,9},{2,10},{3,11},{4,12},{5,13},{6,14},{7,15},{8,0},{9,1},... | collective-permute-start | bytes 3145736 | tf_op jit(solution)/shard_map/ppermute | solution.py:66
  361.2 24.8 %collective-permute-done.4 = f32[32,64,128]{2,0,1:T(8,128)} collective-permute-done((f32[32,64,128]{2,0,1:T(8,128)S(1)}, f32[32,64,128]{2,0,1:T(8,128)}, u32[]{:S(2)}, u32[]{:S(2)}) %collective-permute-start.4) | collective-permute-done | bytes 1048608 | tf_op jit(solution)/shard_map/ppermute | solution.py:66
  (114 shorter events, 120.8 us)
Async XLA Ops:
  0.6 272.1 %copy-start = (bf16[1,64,128,128]{3,2,1,0:T(8,128)(2,1)S(1)}, bf16[1,64,128,128]{3,2,1,0:T(8,128)(2,1)}, u32[]{:S(2)}) copy-start(bf16[1,64,128,128]{3,2,1,0:T(8,128)(2,1)} %param.17) | copy-start | bytes 6291460
  0.6 271.6 %copy-start.5 = (s32[1,64]{1,0:T(1,128)S(1)}, s32[1,64]{1,0:T(1,128)}, u32[]{:S(2)}) copy-start(s32[1,64]{1,0:T(1,128)} %param.15) | copy-start | bytes 772
  1.5 3.5 collective-permute-start
  7.1 5.8 %collective-permute-start = (f32[64,128]{1,0:T(8,128)S(1)}, f32[64,128]{1,0:T(8,128)S(1)}, u32[]{:S(2)}, u32[]{:S(2)}) collective-permute-start(f32[64,128]{1,0:T(8,128)S(1)} %get-tuple-element.79), channel_id=1, source_target_pairs={{16,0},{32,16},{48,32},{64,48},{80,64},{96,80},{112,96},{128,112},... | collective-permute-start | bytes 98312 | tf_op jit(solution)/shard_map/while/body/eval_jaxpr/ppermute | solution.py:12
  15.0 6.4 %collective-permute-start = (f32[64,128]{1,0:T(8,128)S(1)}, f32[64,128]{1,0:T(8,128)S(1)}, u32[]{:S(2)}, u32[]{:S(2)}) collective-permute-start(f32[64,128]{1,0:T(8,128)S(1)} %get-tuple-element.79), channel_id=1, source_target_pairs={{16,0},{32,16},{48,32},{64,48},{80,64},{96,80},{112,96},{128,112},... | collective-permute-start | bytes 98312 | tf_op jit(solution)/shard_map/while/body/eval_jaxpr/ppermute | solution.py:12
  23.5 6.4 %collective-permute-start = (f32[64,128]{1,0:T(8,128)S(1)}, f32[64,128]{1,0:T(8,128)S(1)}, u32[]{:S(2)}, u32[]{:S(2)}) collective-permute-start(f32[64,128]{1,0:T(8,128)S(1)} %get-tuple-element.79), channel_id=1, source_target_pairs={{16,0},{32,16},{48,32},{64,48},{80,64},{96,80},{112,96},{128,112},... | collective-permute-start | bytes 98312 | tf_op jit(solution)/shard_map/while/body/eval_jaxpr/ppermute | solution.py:12
  32.1 6.4 %collective-permute-start = (f32[64,128]{1,0:T(8,128)S(1)}, f32[64,128]{1,0:T(8,128)S(1)}, u32[]{:S(2)}, u32[]{:S(2)}) collective-permute-start(f32[64,128]{1,0:T(8,128)S(1)} %get-tuple-element.79), channel_id=1, source_target_pairs={{16,0},{32,16},{48,32},{64,48},{80,64},{96,80},{112,96},{128,112},... | collective-permute-start | bytes 98312 | tf_op jit(solution)/shard_map/while/body/eval_jaxpr/ppermute | solution.py:12
  40.6 6.4 %collective-permute-start = (f32[64,128]{1,0:T(8,128)S(1)}, f32[64,128]{1,0:T(8,128)S(1)}, u32[]{:S(2)}, u32[]{:S(2)}) collective-permute-start(f32[64,128]{1,0:T(8,128)S(1)} %get-tuple-element.79), channel_id=1, source_target_pairs={{16,0},{32,16},{48,32},{64,48},{80,64},{96,80},{112,96},{128,112},... | collective-permute-start | bytes 98312 | tf_op jit(solution)/shard_map/while/body/eval_jaxpr/ppermute | solution.py:12
  49.1 6.4 %collective-permute-start = (f32[64,128]{1,0:T(8,128)S(1)}, f32[64,128]{1,0:T(8,128)S(1)}, u32[]{:S(2)}, u32[]{:S(2)}) collective-permute-start(f32[64,128]{1,0:T(8,128)S(1)} %get-tuple-element.79), channel_id=1, source_target_pairs={{16,0},{32,16},{48,32},{64,48},{80,64},{96,80},{112,96},{128,112},... | collective-permute-start | bytes 98312 | tf_op jit(solution)/shard_map/while/body/eval_jaxpr/ppermute | solution.py:12
  57.6 6.4 %collective-permute-start = (f32[64,128]{1,0:T(8,128)S(1)}, f32[64,128]{1,0:T(8,128)S(1)}, u32[]{:S(2)}, u32[]{:S(2)}) collective-permute-start(f32[64,128]{1,0:T(8,128)S(1)} %get-tuple-element.79), channel_id=1, source_target_pairs={{16,0},{32,16},{48,32},{64,48},{80,64},{96,80},{112,96},{128,112},... | collective-permute-start | bytes 98312 | tf_op jit(solution)/shard_map/while/body/eval_jaxpr/ppermute | solution.py:12
  66.2 6.4 %collective-permute-start = (f32[64,128]{1,0:T(8,128)S(1)}, f32[64,128]{1,0:T(8,128)S(1)}, u32[]{:S(2)}, u32[]{:S(2)}) collective-permute-start(f32[64,128]{1,0:T(8,128)S(1)} %get-tuple-element.79), channel_id=1, source_target_pairs={{16,0},{32,16},{48,32},{64,48},{80,64},{96,80},{112,96},{128,112},... | collective-permute-start | bytes 98312 | tf_op jit(solution)/shard_map/while/body/eval_jaxpr/ppermute | solution.py:12
  74.7 6.4 %collective-permute-start = (f32[64,128]{1,0:T(8,128)S(1)}, f32[64,128]{1,0:T(8,128)S(1)}, u32[]{:S(2)}, u32[]{:S(2)}) collective-permute-start(f32[64,128]{1,0:T(8,128)S(1)} %get-tuple-element.79), channel_id=1, source_target_pairs={{16,0},{32,16},{48,32},{64,48},{80,64},{96,80},{112,96},{128,112},... | collective-permute-start | bytes 98312 | tf_op jit(solution)/shard_map/while/body/eval_jaxpr/ppermute | solution.py:12
  83.2 6.4 %collective-permute-start = (f32[64,128]{1,0:T(8,128)S(1)}, f32[64,128]{1,0:T(8,128)S(1)}, u32[]{:S(2)}, u32[]{:S(2)}) collective-permute-start(f32[64,128]{1,0:T(8,128)S(1)} %get-tuple-element.79), channel_id=1, source_target_pairs={{16,0},{32,16},{48,32},{64,48},{80,64},{96,80},{112,96},{128,112},... | collective-permute-start | bytes 98312 | tf_op jit(solution)/shard_map/while/body/eval_jaxpr/ppermute | solution.py:12
  91.7 6.4 %collective-permute-start = (f32[64,128]{1,0:T(8,128)S(1)}, f32[64,128]{1,0:T(8,128)S(1)}, u32[]{:S(2)}, u32[]{:S(2)}) collective-permute-start(f32[64,128]{1,0:T(8,128)S(1)} %get-tuple-element.79), channel_id=1, source_target_pairs={{16,0},{32,16},{48,32},{64,48},{80,64},{96,80},{112,96},{128,112},... | collective-permute-start | bytes 98312 | tf_op jit(solution)/shard_map/while/body/eval_jaxpr/ppermute | solution.py:12
  100.3 6.4 %collective-permute-start = (f32[64,128]{1,0:T(8,128)S(1)}, f32[64,128]{1,0:T(8,128)S(1)}, u32[]{:S(2)}, u32[]{:S(2)}) collective-permute-start(f32[64,128]{1,0:T(8,128)S(1)} %get-tuple-element.79), channel_id=1, source_target_pairs={{16,0},{32,16},{48,32},{64,48},{80,64},{96,80},{112,96},{128,112},... | collective-permute-start | bytes 98312 | tf_op jit(solution)/shard_map/while/body/eval_jaxpr/ppermute | solution.py:12
  108.8 6.4 %collective-permute-start = (f32[64,128]{1,0:T(8,128)S(1)}, f32[64,128]{1,0:T(8,128)S(1)}, u32[]{:S(2)}, u32[]{:S(2)}) collective-permute-start(f32[64,128]{1,0:T(8,128)S(1)} %get-tuple-element.79), channel_id=1, source_target_pairs={{16,0},{32,16},{48,32},{64,48},{80,64},{96,80},{112,96},{128,112},... | collective-permute-start | bytes 98312 | tf_op jit(solution)/shard_map/while/body/eval_jaxpr/ppermute | solution.py:12
  117.3 6.4 %collective-permute-start = (f32[64,128]{1,0:T(8,128)S(1)}, f32[64,128]{1,0:T(8,128)S(1)}, u32[]{:S(2)}, u32[]{:S(2)}) collective-permute-start(f32[64,128]{1,0:T(8,128)S(1)} %get-tuple-element.79), channel_id=1, source_target_pairs={{16,0},{32,16},{48,32},{64,48},{80,64},{96,80},{112,96},{128,112},... | collective-permute-start | bytes 98312 | tf_op jit(solution)/shard_map/while/body/eval_jaxpr/ppermute | solution.py:12
  125.8 6.4 %collective-permute-start = (f32[64,128]{1,0:T(8,128)S(1)}, f32[64,128]{1,0:T(8,128)S(1)}, u32[]{:S(2)}, u32[]{:S(2)}) collective-permute-start(f32[64,128]{1,0:T(8,128)S(1)} %get-tuple-element.79), channel_id=1, source_target_pairs={{16,0},{32,16},{48,32},{64,48},{80,64},{96,80},{112,96},{128,112},... | collective-permute-start | bytes 98312 | tf_op jit(solution)/shard_map/while/body/eval_jaxpr/ppermute | solution.py:12
  134.4 6.4 %collective-permute-start = (f32[64,128]{1,0:T(8,128)S(1)}, f32[64,128]{1,0:T(8,128)S(1)}, u32[]{:S(2)}, u32[]{:S(2)}) collective-permute-start(f32[64,128]{1,0:T(8,128)S(1)} %get-tuple-element.79), channel_id=1, source_target_pairs={{16,0},{32,16},{48,32},{64,48},{80,64},{96,80},{112,96},{128,112},... | collective-permute-start | bytes 98312 | tf_op jit(solution)/shard_map/while/body/eval_jaxpr/ppermute | solution.py:12
  142.9 6.4 %collective-permute-start = (f32[64,128]{1,0:T(8,128)S(1)}, f32[64,128]{1,0:T(8,128)S(1)}, u32[]{:S(2)}, u32[]{:S(2)}) collective-permute-start(f32[64,128]{1,0:T(8,128)S(1)} %get-tuple-element.79), channel_id=1, source_target_pairs={{16,0},{32,16},{48,32},{64,48},{80,64},{96,80},{112,96},{128,112},... | collective-permute-start | bytes 98312 | tf_op jit(solution)/shard_map/while/body/eval_jaxpr/ppermute | solution.py:12
  151.4 6.4 %collective-permute-start = (f32[64,128]{1,0:T(8,128)S(1)}, f32[64,128]{1,0:T(8,128)S(1)}, u32[]{:S(2)}, u32[]{:S(2)}) collective-permute-start(f32[64,128]{1,0:T(8,128)S(1)} %get-tuple-element.79), channel_id=1, source_target_pairs={{16,0},{32,16},{48,32},{64,48},{80,64},{96,80},{112,96},{128,112},... | collective-permute-start | bytes 98312 | tf_op jit(solution)/shard_map/while/body/eval_jaxpr/ppermute | solution.py:12
  159.9 6.4 %collective-permute-start = (f32[64,128]{1,0:T(8,128)S(1)}, f32[64,128]{1,0:T(8,128)S(1)}, u32[]{:S(2)}, u32[]{:S(2)}) collective-permute-start(f32[64,128]{1,0:T(8,128)S(1)} %get-tuple-element.79), channel_id=1, source_target_pairs={{16,0},{32,16},{48,32},{64,48},{80,64},{96,80},{112,96},{128,112},... | collective-permute-start | bytes 98312 | tf_op jit(solution)/shard_map/while/body/eval_jaxpr/ppermute | solution.py:12
  168.4 6.4 %collective-permute-start = (f32[64,128]{1,0:T(8,128)S(1)}, f32[64,128]{1,0:T(8,128)S(1)}, u32[]{:S(2)}, u32[]{:S(2)}) collective-permute-start(f32[64,128]{1,0:T(8,128)S(1)} %get-tuple-element.79), channel_id=1, source_target_pairs={{16,0},{32,16},{48,32},{64,48},{80,64},{96,80},{112,96},{128,112},... | collective-permute-start | bytes 98312 | tf_op jit(solution)/shard_map/while/body/eval_jaxpr/ppermute | solution.py:12
  177.0 6.4 %collective-permute-start = (f32[64,128]{1,0:T(8,128)S(1)}, f32[64,128]{1,0:T(8,128)S(1)}, u32[]{:S(2)}, u32[]{:S(2)}) collective-permute-start(f32[64,128]{1,0:T(8,128)S(1)} %get-tuple-element.79), channel_id=1, source_target_pairs={{16,0},{32,16},{48,32},{64,48},{80,64},{96,80},{112,96},{128,112},... | collective-permute-start | bytes 98312 | tf_op jit(solution)/shard_map/while/body/eval_jaxpr/ppermute | solution.py:12
  185.5 6.4 %collective-permute-start = (f32[64,128]{1,0:T(8,128)S(1)}, f32[64,128]{1,0:T(8,128)S(1)}, u32[]{:S(2)}, u32[]{:S(2)}) collective-permute-start(f32[64,128]{1,0:T(8,128)S(1)} %get-tuple-element.79), channel_id=1, source_target_pairs={{16,0},{32,16},{48,32},{64,48},{80,64},{96,80},{112,96},{128,112},... | collective-permute-start | bytes 98312 | tf_op jit(solution)/shard_map/while/body/eval_jaxpr/ppermute | solution.py:12
  194.0 6.4 %collective-permute-start = (f32[64,128]{1,0:T(8,128)S(1)}, f32[64,128]{1,0:T(8,128)S(1)}, u32[]{:S(2)}, u32[]{:S(2)}) collective-permute-start(f32[64,128]{1,0:T(8,128)S(1)} %get-tuple-element.79), channel_id=1, source_target_pairs={{16,0},{32,16},{48,32},{64,48},{80,64},{96,80},{112,96},{128,112},... | collective-permute-start | bytes 98312 | tf_op jit(solution)/shard_map/while/body/eval_jaxpr/ppermute | solution.py:12
  202.5 6.4 %collective-permute-start = (f32[64,128]{1,0:T(8,128)S(1)}, f32[64,128]{1,0:T(8,128)S(1)}, u32[]{:S(2)}, u32[]{:S(2)}) collective-permute-start(f32[64,128]{1,0:T(8,128)S(1)} %get-tuple-element.79), channel_id=1, source_target_pairs={{16,0},{32,16},{48,32},{64,48},{80,64},{96,80},{112,96},{128,112},... | collective-permute-start | bytes 98312 | tf_op jit(solution)/shard_map/while/body/eval_jaxpr/ppermute | solution.py:12
  211.1 6.4 %collective-permute-start = (f32[64,128]{1,0:T(8,128)S(1)}, f32[64,128]{1,0:T(8,128)S(1)}, u32[]{:S(2)}, u32[]{:S(2)}) collective-permute-start(f32[64,128]{1,0:T(8,128)S(1)} %get-tuple-element.79), channel_id=1, source_target_pairs={{16,0},{32,16},{48,32},{64,48},{80,64},{96,80},{112,96},{128,112},... | collective-permute-start | bytes 98312 | tf_op jit(solution)/shard_map/while/body/eval_jaxpr/ppermute | solution.py:12
  219.6 6.4 %collective-permute-start = (f32[64,128]{1,0:T(8,128)S(1)}, f32[64,128]{1,0:T(8,128)S(1)}, u32[]{:S(2)}, u32[]{:S(2)}) collective-permute-start(f32[64,128]{1,0:T(8,128)S(1)} %get-tuple-element.79), channel_id=1, source_target_pairs={{16,0},{32,16},{48,32},{64,48},{80,64},{96,80},{112,96},{128,112},... | collective-permute-start | bytes 98312 | tf_op jit(solution)/shard_map/while/body/eval_jaxpr/ppermute | solution.py:12
  228.1 6.4 %collective-permute-start = (f32[64,128]{1,0:T(8,128)S(1)}, f32[64,128]{1,0:T(8,128)S(1)}, u32[]{:S(2)}, u32[]{:S(2)}) collective-permute-start(f32[64,128]{1,0:T(8,128)S(1)} %get-tuple-element.79), channel_id=1, source_target_pairs={{16,0},{32,16},{48,32},{64,48},{80,64},{96,80},{112,96},{128,112},... | collective-permute-start | bytes 98312 | tf_op jit(solution)/shard_map/while/body/eval_jaxpr/ppermute | solution.py:12
  236.6 6.4 %collective-permute-start = (f32[64,128]{1,0:T(8,128)S(1)}, f32[64,128]{1,0:T(8,128)S(1)}, u32[]{:S(2)}, u32[]{:S(2)}) collective-permute-start(f32[64,128]{1,0:T(8,128)S(1)} %get-tuple-element.79), channel_id=1, source_target_pairs={{16,0},{32,16},{48,32},{64,48},{80,64},{96,80},{112,96},{128,112},... | collective-permute-start | bytes 98312 | tf_op jit(solution)/shard_map/while/body/eval_jaxpr/ppermute | solution.py:12
  245.2 6.4 %collective-permute-start = (f32[64,128]{1,0:T(8,128)S(1)}, f32[64,128]{1,0:T(8,128)S(1)}, u32[]{:S(2)}, u32[]{:S(2)}) collective-permute-start(f32[64,128]{1,0:T(8,128)S(1)} %get-tuple-element.79), channel_id=1, source_target_pairs={{16,0},{32,16},{48,32},{64,48},{80,64},{96,80},{112,96},{128,112},... | collective-permute-start | bytes 98312 | tf_op jit(solution)/shard_map/while/body/eval_jaxpr/ppermute | solution.py:12
  253.7 6.4 %collective-permute-start = (f32[64,128]{1,0:T(8,128)S(1)}, f32[64,128]{1,0:T(8,128)S(1)}, u32[]{:S(2)}, u32[]{:S(2)}) collective-permute-start(f32[64,128]{1,0:T(8,128)S(1)} %get-tuple-element.79), channel_id=1, source_target_pairs={{16,0},{32,16},{48,32},{64,48},{80,64},{96,80},{112,96},{128,112},... | collective-permute-start | bytes 98312 | tf_op jit(solution)/shard_map/while/body/eval_jaxpr/ppermute | solution.py:12
  262.2 6.4 %collective-permute-start = (f32[64,128]{1,0:T(8,128)S(1)}, f32[64,128]{1,0:T(8,128)S(1)}, u32[]{:S(2)}, u32[]{:S(2)}) collective-permute-start(f32[64,128]{1,0:T(8,128)S(1)} %get-tuple-element.79), channel_id=1, source_target_pairs={{16,0},{32,16},{48,32},{64,48},{80,64},{96,80},{112,96},{128,112},... | collective-permute-start | bytes 98312 | tf_op jit(solution)/shard_map/while/body/eval_jaxpr/ppermute | solution.py:12
  270.7 3.2 copy-start.2
  272.2 1.8 copy-start.1
  272.7 1.3 copy-start.6
  276.0 25.1 %collective-permute-start.1 = (f32[32,64,128]{2,0,1:T(8,128)S(1)}, f32[32,64,128]{2,0,1:T(8,128)S(1)}, u32[]{:S(2)}, u32[]{:S(2)}) collective-permute-start(f32[32,64,128]{2,0,1:T(8,128)S(1)} %fusion.2), channel_id=1, source_target_pairs={{0,1},{1,0},{2,3},{3,2},{4,5},{5,4},{6,7},{7,6},{8,9},{9,8},{10,11... | collective-permute-start | bytes 3145736 | tf_op jit(solution)/shard_map/ppermute | solution.py:66
  301.3 27.7 %collective-permute-start.2 = (f32[32,64,128]{2,0,1:T(8,128)S(1)}, f32[32,64,128]{2,0,1:T(8,128)S(1)}, u32[]{:S(2)}, u32[]{:S(2)}) collective-permute-start(f32[32,64,128]{2,0,1:T(8,128)S(1)} %add.18), channel_id=1, source_target_pairs={{0,2},{1,3},{2,0},{3,1},{4,6},{5,7},{6,4},{7,5},{8,10},{9,11},{10,... | collective-permute-start | bytes 3145736 | tf_op jit(solution)/shard_map/ppermute | solution.py:66
  329.3 56.7 %copy-start.4 = (bf16[1,2,64,128]{3,2,1,0:T(8,128)(2,1)S(1)}, bf16[1,2,64,128]{3,2,1,0:T(8,128)(2,1)}, u32[]{:S(2)}) copy-start(bf16[1,2,64,128]{3,2,1,0:T(8,128)(2,1)} %param.22) | copy-start | bytes 98308
  329.3 57.7 %copy-start.3 = (bf16[1,2,128,128]{3,2,1,0:T(8,128)(2,1)S(1)}, bf16[1,2,128,128]{3,2,1,0:T(8,128)(2,1)}, u32[]{:S(2)}) copy-start(bf16[1,2,128,128]{3,2,1,0:T(8,128)(2,1)} %param.21) | copy-start | bytes 196612
  329.3 27.5 %collective-permute-start.3 = (f32[32,64,128]{2,0,1:T(8,128)S(1)}, f32[32,64,128]{2,0,1:T(8,128)S(1)}, u32[]{:S(2)}, u32[]{:S(2)}) collective-permute-start(f32[32,64,128]{2,0,1:T(8,128)S(1)} %add.19), channel_id=1, source_target_pairs={{0,4},{1,5},{2,6},{3,7},{4,0},{5,1},{6,2},{7,3},{8,12},{9,13},{10,... | collective-permute-start | bytes 3145736 | tf_op jit(solution)/shard_map/ppermute | solution.py:66
  357.0 29.0 %collective-permute-start.4 = (f32[32,64,128]{2,0,1:T(8,128)S(1)}, f32[32,64,128]{2,0,1:T(8,128)}, u32[]{:S(2)}, u32[]{:S(2)}) collective-permute-start(f32[32,64,128]{2,0,1:T(8,128)S(1)} %add.20), channel_id=1, source_target_pairs={{0,8},{1,9},{2,10},{3,11},{4,12},{5,13},{6,14},{7,15},{8,0},{9,1},... | collective-permute-start | bytes 3145736 | tf_op jit(solution)/shard_map/ppermute | solution.py:66
